TPU v7x, 32 devices: a whole 2x2x4 slice. The times are simulated.
32 devices in a mesh: dp: 2 (over y), row: 4 (over x, core), col: 4 (over z).
Axes of the slice: x: 2, y: 2, z: 4, core: 2. Of those that a mesh axis runs over, the one named last changes fastest.
Arguments:
- patches: bfloat16 [2, 512, 1456], P('dp', 'col', 'row'), may hold values from -6 to 6
- queries: bfloat16 [2, 512, 6144], P('dp', 'col', 'row'), may hold values from -6 to 6
- attn_keys: bfloat16 [2, 512, 6144], P('dp', 'col', 'row'), may hold values from -6 to 6
- attn_values: bfloat16 [2, 512, 6144], P('dp', 'col', 'row'), may hold values from -6 to 6
- out_weight: bfloat16 [6144, 12288], P('row', 'col'), may hold values from -0.15625 to 0.15625
- output_grad: bfloat16 [2, 512, 12288], P('dp', 'row', 'col'), may hold values from -4 to 4
Outputs:
- query_grad: float32 [2, 512, 6144], P('dp', 'col', 'row')
- key_grad: float32 [2, 512, 6144], P('dp', 'col', 'row')
- value_grad: float32 [2, 512, 6144], P('dp', 'col', 'row')
- out_weight_grad: float32 [6144, 12288], P('row', 'col')
- embed_weight_grad: float32 [1456, 12288], P('row', 'col')
All inputs are finite; a program needn't handle non-finite values.
Results may differ from a plain program's by a relative error of at most 0.025.
Values may be sent and summed in bfloat16 or wider, within the bound.
No kernel may reach another device: no remote copies, remote signals or barrier semaphores. Data moves between devices by JAX's collectives and lax.ppermute only.
A program may use at most 128 MiB of HBM per device.

v0:
```python
import jax
import jax.numpy as jnp
from jax import lax
from jax.sharding import PartitionSpec as P

DH = 128


def contract_rows(left, right):
    return lax.dot_general(
        left, right, (((0,), (0,)), ((), ())), preferred_element_type=jnp.float32
    )


def body(patches, queries, attn_keys, attn_values, out_weight, output_grad):
    factor = DH ** (-0.5)
    local_rows = queries.shape[1]
    feature_width = queries.shape[2]
    head_count = feature_width // DH
    every_key, every_value, every_patch = (
        lax.all_gather(attn_keys, "col", axis=1, tiled=True),
        lax.all_gather(attn_values, "col", axis=1, tiled=True),
        lax.all_gather(patches, "col", axis=1, tiled=True),
    )
    local_query = queries[0].reshape(local_rows, head_count, DH)
    all_keys = every_key[0].reshape(-1, head_count, DH)
    all_values = every_value[0].reshape(-1, head_count, DH)
    scores = (
        jnp.einsum("qhd,khd->hqk", local_query, all_keys, preferred_element_type=jnp.float32)
        * factor
    )
    row_max = jnp.max(scores, axis=2, keepdims=True)
    log_total = row_max + jnp.log(jnp.sum(jnp.exp(scores - row_max), axis=2, keepdims=True))
    attn_probs = jnp.exp(scores - log_total).astype(jnp.bfloat16)
    attn_out = jnp.einsum(
        "hqk,khd->qhd", attn_probs, all_values, preferred_element_type=jnp.float32
    ).astype(jnp.bfloat16)
    out_local = attn_out.reshape(1, local_rows, feature_width)
    dense_grad = lax.all_gather(output_grad, "row", axis=1, tiled=True)[0]
    attn_grad = lax.psum_scatter(
        lax.dot_general(
            dense_grad, out_weight, (((1,), (1,)), ((), ())), preferred_element_type=jnp.float32
        ),
        "col",
        scatter_dimension=0,
        tiled=True,
    ).astype(jnp.bfloat16)
    grad_heads = attn_grad.reshape(local_rows, head_count, DH)
    prob_grad = jnp.einsum(
        "qhd,khd->hqk", grad_heads, all_values, preferred_element_type=jnp.float32
    )
    row_dot = jnp.transpose(
        jnp.sum(grad_heads.astype(jnp.float32) * attn_out.astype(jnp.float32), axis=2)
    )[:, :, None]
    score_grad = (attn_probs.astype(jnp.float32) * (prob_grad - row_dot)).astype(jnp.bfloat16)
    query_grad = (
        jnp.einsum("hqk,khd->qhd", score_grad, all_keys, preferred_element_type=jnp.float32)
        * factor
    )
    every_out = lax.all_gather(out_local, "col", axis=1, tiled=True)
    key_term = (
        jnp.einsum("hqk,qhd->khd", score_grad, local_query, preferred_element_type=jnp.float32)
        * factor
    )
    value_term = jnp.einsum(
        "hqk,qhd->khd", attn_probs, grad_heads, preferred_element_type=jnp.float32
    )
    key_sum, value_sum = (
        lax.psum_scatter(
            key_term.reshape(-1, feature_width).astype(jnp.bfloat16),
            "col",
            scatter_dimension=0,
            tiled=True,
        ).astype(jnp.float32),
        lax.psum_scatter(
            value_term.reshape(-1, feature_width).astype(jnp.bfloat16),
            "col",
            scatter_dimension=0,
            tiled=True,
        ).astype(jnp.float32),
    )
    out_part = contract_rows(every_out[0], dense_grad)
    embed_part = contract_rows(every_patch[0], dense_grad)
    out_weight_grad, embed_weight_grad = (
        lax.psum(out_part.astype(jnp.bfloat16), "dp").astype(jnp.float32),
        lax.psum(embed_part.astype(jnp.bfloat16), "dp").astype(jnp.float32),
    )
    return (
        query_grad.reshape(1, local_rows, feature_width),
        key_sum.reshape(1, local_rows, feature_width),
        value_sum.reshape(1, local_rows, feature_width),
        out_weight_grad,
        embed_weight_grad,
    )


def solution(mesh):
    placed = (
        P("dp", "col", "row"),
        P("dp", "col", "row"),
        P("dp", "col", "row"),
        P("dp", "col", "row"),
        P("row", "col"),
        P("dp", "row", "col"),
    )
    return jax.shard_map(
        body,
        mesh=mesh,
        in_specs=placed,
        out_specs=(
            P("dp", "col", "row"),
            P("dp", "col", "row"),
            P("dp", "col", "row"),
            P("row", "col"),
            P("row", "col"),
        ),
        check_vma=False,
    )
```

profile of v0, /device:TPU:0, one launch (start us, length us, event | category | flops | bytes accessed | tf_op | source)
XLA Modules:
  0.0 593.3 jit_solution(1535676170303104737)
XLA Ops:
  7.2 0.0 all-gather.7.cloned.1.call-start
  7.2 0.7 all-gather.7.cloned.1.call-update
  7.9 0.0 all-gather.5.cloned.1.call-start
  7.9 1.9 copy.22
  9.9 0.0 all-gather.5.cloned.1.call-update
  9.9 0.0 reduce-scatter.4.cloned.1.call-start
  9.9 30.9 %all-gather.7.cloned.1.call-done = bf16[1,512,3072]{2,1,0:T(8,128)(2,1)} async-done(((bf16[1,128,3072]{2,1,0:T(8,128)(2,1)}), bf16[1,512,3072]{2,1,0:T(8,128)(2,1)}) %all-gather.7.cloned.1.call-update) | async-done | bytes 3145744 | tf_op jit(solution)/shard_map/all_gather | solution.py:39
  40.8 10.6 %fusion.2 = f32[512,1536]{1,0:T(8,128)} fusion(bf16[1536,3072]{1,0:T(8,128)(2,1)} %param.10, bf16[1,512,3072]{2,1,0:T(8,128)(2,1)} %all-gather.7.cloned.1.call-done), kind=kOutput, calls=%fused_computation.4 | convolution fusion | flops 4831838208 | bytes 15728640 | tf_op jit(solution)/shard_map/dot_general | solution.py:41
  51.4 0.0 copy-start.3
  51.4 0.0 copy-start.4
  51.4 0.0 reduce-scatter.4.cloned.1.call-update
  51.4 0.0 all-gather.9.cloned.1.call-start
  51.5 0.9 copy-done.3
  52.4 0.9 copy.26
  53.3 0.0 all-gather.9.cloned.1.call-update
  53.4 0.0 all-gather.11.cloned.1.call-start
  53.4 0.0 copy-done.4
  53.4 0.2 copy.21
  53.6 0.0 copy-start.1
  53.7 27.0 %all-gather.5.cloned.1.call-done = bf16[1,512,1536]{1,2,0:T(8,128)(2,1)} async-done(((bf16[1,128,1536]{1,2,0:T(8,128)(2,1)}), bf16[1,512,1536]{1,2,0:T(8,128)(2,1)}) %all-gather.5.cloned.1.call-update) | async-done | bytes 1572880 | tf_op jit(solution)/shard_map/all_gather | solution.py:21
  80.7 2.1 multiply_reduce_fusion
  82.8 1.0 exponential_reduce_fusion
  83.8 0.0 copy-done.1
  83.8 0.5 exponential_convert_fusion
  84.4 57.7 %reduce-scatter.4.cloned.1.call-done = f32[128,1536]{1,0:T(8,128)} async-done(((f32[512,1536]{1,0:T(8,128)}), f32[128,1536]{1,0:T(8,128)}) %reduce-scatter.4.cloned.1.call-update) | async-done | bytes 786448 | tf_op jit(solution)/shard_map/reduce_scatter | solution.py:40
  142.1 1.2 convert_element_type.58
  143.3 0.2 copy.25
  143.5 38.4 %all-gather.9.cloned.1.call-done = bf16[1,512,1536]{1,2,0:T(8,128)(2,1)} async-done(((bf16[1,128,1536]{1,2,0:T(8,128)(2,1)}), bf16[1,512,1536]{1,2,0:T(8,128)(2,1)}) %all-gather.9.cloned.1.call-update) | async-done | bytes 1572880 | tf_op jit(solution)/shard_map/all_gather | solution.py:22
  181.9 2.7 multiply_reduce_fusion.1
  184.6 0.0 all-gather.11.cloned.1.call-update
  184.6 0.0 reduce-scatter.6.cloned.1.call-start
  184.7 2.0 multiply_convert_fusion.1
  186.7 2.7 multiply_convert_fusion
  189.4 2.7 copy.29
  192.1 0.0 reduce-scatter.6.cloned.1.call-update
  192.1 0.0 reduce-scatter.8.cloned.1.call-start
  192.1 1.7 convolution_convert_fusion.2
  193.8 0.0 copy-start.5
  193.8 2.6 copy.30
  196.5 0.0 reduce-scatter.8.cloned.1.call-update
  196.5 0.0 all-reduce.3.cloned.1.call-start
  196.6 0.0 copy-done.5
  196.6 20.1 %all_gather.19 = bf16[1,512,364]{1,2,0:T(8,128)(2,1)S(1)} all-gather(bf16[1,128,364]{1,2,0:T(8,128)(2,1)S(1)} %copy-done.5), channel_id=1, replica_groups=mesh['dp'=2,'row'=4,'col'=4] {'col'}, dimensions={1}, use_global_device_ids=true | all-gather | bytes 465920 | tf_op jit(solution)/shard_map/all_gather | solution.py:23
  216.7 4.6 convolution_convert_fusion.1
  221.3 5.5 all-gather.11.cloned.1.call-done
  226.8 9.3 %convolution_convert_fusion = bf16[1536,3072]{1,0:T(8,128)(2,1)} fusion(bf16[1,512,3072]{2,1,0:T(8,128)(2,1)} %all-gather.7.cloned.1.call-done, bf16[1,512,1536]{1,2,0:T(8,128)(2,1)} %all-gather.11.cloned.1.call-done), kind=kOutput, calls=%fused_computation | convolution fusion | flops 4836556800 | bytes 14155776 | tf_op jit(solution)/shard_map/dot_general | solution.py:10
  236.1 0.0 copy-start
  236.1 0.0 all-reduce.3.cloned.1.call-update
  236.1 1.4 copy-done
  237.5 1.5 convolution_multiply_fusion
  238.9 2.3 copy.31
  241.2 21.2 %reduce-scatter.6.cloned.1.call-done = bf16[128,1536]{1,0:T(8,128)(2,1)} async-done(((bf16[512,1536]{1,0:T(8,128)(2,1)}), bf16[128,1536]{1,0:T(8,128)(2,1)}) %reduce-scatter.6.cloned.1.call-update) | async-done | bytes 393232 | tf_op jit(solution)/shard_map/reduce_scatter | solution.py:69
  262.4 2.0 bitcast_convert_fusion.1
  264.4 34.6 %reduce-scatter.8.cloned.1.call-done = bf16[128,1536]{1,0:T(8,128)(2,1)} async-done(((bf16[512,1536]{1,0:T(8,128)(2,1)}), bf16[128,1536]{1,0:T(8,128)(2,1)}) %reduce-scatter.8.cloned.1.call-update) | async-done | bytes 393232 | tf_op jit(solution)/shard_map/reduce_scatter | solution.py:75
  299.0 2.0 bitcast_convert_fusion
  301.0 270.0 %all-reduce.3.cloned.1.call-done = (bf16[1536,3072]{1,0:T(8,128)(2,1)}, bf16[364,3072]{1,0:T(8,128)(2,1)}) async-done(((bf16[1536,3072]{1,0:T(8,128)(2,1)}, bf16[364,3072]{1,0:T(8,128)(2,1)}), (bf16[1536,3072]{1,0:T(8,128)(2,1)}, bf16[364,3072]{1,0:T(8,128)(2,1)})) %all-reduce.3.cloned.1.call-update) | async-done | bytes 11673616 | tf_op jit(solution)/shard_map/psum | solution.py:85
  571.0 0.0 copy-start.2
  571.0 12.9 %convert_element_type.71 = f32[1536,3072]{1,0:T(8,128)} convert(bf16[1536,3072]{1,0:T(8,128)(2,1)} %get-tuple-element.15) | non-fusion elementwise | flops 4718592 | bytes 28311552 | tf_op jit(solution)/shard_map/convert_element_type | solution.py:85
  583.8 0.0 copy-done.2
  583.8 2.7 convert_element_type.73
  (1 shorter events, 0.0 us)
Async XLA Ops:
  7.2 33.7 %all-gather.7.cloned.1.call-start = ((), (), s32[]{:S(2)}) async-start(), calls=%async_computation.4 | async-start | bytes 3932160 | tf_op jit(solution)/shard_map/all_gather | solution.py:39
  7.9 72.8 %all-gather.5.cloned.1.call-start = ((), (), s32[]{:S(2)}) async-start(), calls=%async_computation.3 | async-start | bytes 1966080 | tf_op jit(solution)/shard_map/all_gather | solution.py:21
  9.9 132.2 %reduce-scatter.4.cloned.1.call-start = ((), (), s32[]{:S(2)}) async-start(), calls=%async_computation.5 | async-start | bytes 3932160 | tf_op jit(solution)/shard_map/reduce_scatter | solution.py:40
  51.4 1.0 copy-start.3
  51.4 2.0 copy-start.4
  51.4 130.4 %all-gather.9.cloned.1.call-start = ((), (), s32[]{:S(2)}) async-start(), calls=%async_computation.6 | async-start | bytes 1966080 | tf_op jit(solution)/shard_map/all_gather | solution.py:22
  53.4 173.4 %all-gather.11.cloned.1.call-start = ((), (), s32[]{:S(2)}) async-start(), calls=%async_computation.9 | async-start | bytes 1966080 | tf_op jit(solution)/shard_map/all_gather | solution.py:60
  53.6 30.2 %copy-start.1 = (bf16[1,128,1536]{1,2,0:T(8,128)(2,1)}, bf16[1,128,1536]{1,2,0:T(8,128)(2,1)S(1)}, u32[]{:S(2)}) copy-start(bf16[1,128,1536]{1,2,0:T(8,128)(2,1)S(1)} %copy.21) | copy-start | bytes 1179652
  184.6 77.8 %reduce-scatter.6.cloned.1.call-start = ((), (), s32[]{:S(2)}) async-start(), calls=%async_computation.7 | async-start | bytes 1966080 | tf_op jit(solution)/shard_map/reduce_scatter | solution.py:69
  192.1 106.9 %reduce-scatter.8.cloned.1.call-start = ((), (), s32[]{:S(2)}) async-start(), calls=%async_computation.8 | async-start | bytes 1966080 | tf_op jit(solution)/shard_map/reduce_scatter | solution.py:75
  193.8 2.7 copy-start.5
  196.5 374.5 %all-reduce.3.cloned.1.call-start = ((), (), s32[]{:S(2)}) async-start(), calls=%async_computation.10 | async-start | bytes 23396352 | tf_op jit(solution)/shard_map/psum | solution.py:85
  236.1 1.4 copy-start
  571.0 12.9 %copy-start.2 = (bf16[364,3072]{1,0:T(8,128)(2,1)S(1)}, bf16[364,3072]{1,0:T(8,128)(2,1)}, u32[]{:S(2)}) copy-start(bf16[364,3072]{1,0:T(8,128)(2,1)} %get-tuple-element.16) | copy-start | bytes 6709252
Sparse Core Ops, SparseCore 0:
  9.6 31.2 all-gather.6
  43.0 37.7 all-gather.4
  83.6 58.4 reduce-scatter.3
  144.1 37.7 all-gather.8
  184.7 41.9 all-gather.10
  228.9 33.4 reduce-scatter.5
  264.7 34.2 reduce-scatter.7
  302.1 268.8 all-reduce.2
where the time goes:
time: 594 us; the launch traced here: 593 us
  waiting for transfers between devices  486 us (82%)
  matrix products  37.2 us (6%)
  other arithmetic  22.1 us (4%)
  blocking collectives  20.1 us (3%)
  between operations  14.2 us (2%)
  local copies, waits for them, and re-layouts  13.2 us (2%)
    psum x1, waiting for transfers between devices, body(): lax.psum(out_part.astype(jnp.bfloat16), 'dp').astype(jnp.float32)  270 us
    reduce_scatter x1, waiting for transfers between devices, body(): lax.psum_scatter(lax.dot_general(dense_grad, out_weight, (((1,), (1,)), (...  57.7 us
    all_gather x1, waiting for transfers between devices, body(): lax.all_gather(attn_values, 'col', axis=1, tiled=True)  38.4 us
    reduce_scatter x1, waiting for transfers between devices, body(): lax.psum_scatter(value_term.reshape(-1, feature_width).astype(jnp.bfloat1...  34.6 us
    all_gather x1, waiting for transfers between devices, body(): dense_grad = lax.all_gather(output_grad, 'row', axis=1, tiled=True)[0]  30.9 us
    all_gather x1, waiting for transfers between devices, body(): lax.all_gather(attn_keys, 'col', axis=1, tiled=True)  27 us
    reduce_scatter x1, waiting for transfers between devices, body(): lax.psum_scatter(key_term.reshape(-1, feature_width).astype(jnp.bfloat16)...  21.2 us
    all_gather x1, blocking collectives, body(): lax.all_gather(patches, 'col', axis=1, tiled=True)  20.1 us
  transfers between devices with their start and end apart: 8, of which 8 were waited for; matrix products, arithmetic and copies ran while one was open for 9% of the time, Pallas kernels for 0%

commit v1 on v0

--- a/solution.py
+++ b/solution.py
@@ -4,6 +4,23 @@
 from jax.sharding import PartitionSpec as P
 
 DH = 128
+
+
+def in_order(blocks, dim):
+    blocks = jnp.moveaxis(blocks, 0, dim)
+    dims = blocks.shape
+    return blocks.reshape(*dims[:dim], dims[dim] * dims[dim + 1], *dims[dim + 2 :])
+
+
+def gather_around(x, axis, dim):
+    peers = lax.axis_size(axis)
+    right = [(i, (i + 1) % peers) for i in range(peers)]
+    pieces = [x]
+    while len(pieces) < peers:
+        pieces.append(lax.ppermute(pieces[-1], axis, right))
+    index = lax.axis_index(axis)
+    pieces = jnp.stack(pieces)[(index - jnp.arange(peers)) % peers]
+    return in_order(pieces, dim)
 
 
 def contract_rows(left, right):
@@ -19,7 +36,7 @@
     head_count = feature_width // DH
     every_key, every_value, every_patch = (
         lax.all_gather(attn_keys, "col", axis=1, tiled=True),
-        lax.all_gather(attn_values, "col", axis=1, tiled=True),
+        gather_around(attn_values, "col", 1),
         lax.all_gather(patches, "col", axis=1, tiled=True),
     )
     local_query = queries[0].reshape(local_rows, head_count, DH)

time: 594 us -> 574 us (0.966)
  waiting for transfers between devices: 486 us -> 458 us
  local copies, waits for them, and re-layouts: 13.2 us -> 19.2 us
    ppermute x0 -> x3, waiting for transfers between devices: none -> 56.8 us  [gather_around(): pieces.append(lax.ppermute(pieces[-1], axis, right))]
    all_gather x1 -> x0, waiting for transfers between devices: 38.4 us -> none  [body(): lax.all_gather(attn_values, 'col', axis=1, tiled=True)]
    all_gather x1, waiting for transfers between devices: 27 us -> 0.02 us  [body(): lax.all_gather(attn_keys, 'col', axis=1, tiled=True)]
    reduce_scatter x1, waiting for transfers between devices: 57.7 us -> 39.5 us  [body(): lax.psum_scatter(lax.dot_general(dense_grad, out_weight, (((1,), (1,)), (...]
  transfers between devices with their start and end apart: 8 -> 10, of which waited for: 8 -> 9; matrix products, arithmetic and copies ran while one was open for 9% -> 10% of each run, Pallas kernels for 0% -> 0%
where the time goes in v1:
time: 574 us
  waiting for transfers between devices  458 us (80%)
  matrix products  35.4 us (6%)
  other arithmetic  23.1 us (4%)
  blocking collectives  20.2 us (4%)
  local copies, waits for them, and re-layouts  19.2 us (3%)
  between operations  14.3 us (2%)
    psum x1, waiting for transfers between devices, body(): lax.psum(out_part.astype(jnp.bfloat16), 'dp').astype(jnp.float32)  270 us
    ppermute x3, waiting for transfers between devices, gather_around(): pieces.append(lax.ppermute(pieces[-1], axis, right))  56.8 us
    reduce_scatter x1, waiting for transfers between devices, body(): lax.psum_scatter(lax.dot_general(dense_grad, out_weight, (((1,), (1,)), (...  39.5 us
    reduce_scatter x1, waiting for transfers between devices, body(): lax.psum_scatter(value_term.reshape(-1, feature_width).astype(jnp.bfloat1...  34.5 us
    all_gather x1, waiting for transfers between devices, body(): dense_grad = lax.all_gather(output_grad, 'row', axis=1, tiled=True)[0]  30.9 us
    reduce_scatter x1, waiting for transfers between devices, body(): lax.psum_scatter(key_term.reshape(-1, feature_width).astype(jnp.bfloat16)...  21.2 us
    all_gather x1, blocking collectives, body(): lax.all_gather(patches, 'col', axis=1, tiled=True)  20.2 us
    dot_general x2, matrix products, contract_rows(): lax.dot_general(left, right, (((0,), (0,)), ((), ())), preferred_element_...  13.9 us
  transfers between devices with their start and end apart: 10, of which 9 were waited for; matrix products, arithmetic and copies ran while one was open for 10% of the time, Pallas kernels for 0%

profile of v1, /device:TPU:0, one launch (start us, length us, event | category | flops | bytes accessed | tf_op | source)
XLA Modules:
  0.0 573.8 jit_solution(15533756566897115436)
XLA Ops:
  7.2 0.0 all-gather.6.cloned.1.call-start
  7.2 0.7 all-gather.6.cloned.1.call-update
  7.9 0.0 all-gather.4.cloned.1.call-start
  7.9 1.9 copy.23
  9.9 0.0 all-gather.4.cloned.1.call-update
  9.9 0.0 reduce-scatter.4.cloned.1.call-start
  9.9 30.9 %all-gather.6.cloned.1.call-done = bf16[1,512,3072]{2,1,0:T(8,128)(2,1)} async-done(((bf16[1,128,3072]{2,1,0:T(8,128)(2,1)}), bf16[1,512,3072]{2,1,0:T(8,128)(2,1)}) %all-gather.6.cloned.1.call-update) | async-done | bytes 3145744 | tf_op jit(solution)/shard_map/all_gather | solution.py:56
  40.8 10.6 %fusion.2 = f32[512,1536]{1,0:T(8,128)} fusion(bf16[1536,3072]{1,0:T(8,128)(2,1)} %param.10, bf16[1,512,3072]{2,1,0:T(8,128)(2,1)} %all-gather.6.cloned.1.call-done), kind=kOutput, calls=%fused_computation.5 | convolution fusion | flops 4831838208 | bytes 15728640 | tf_op jit(solution)/shard_map/dot_general | solution.py:58
  51.4 0.0 reduce-scatter.4.cloned.1.call-update
  51.4 0.0 all-gather.8.cloned.1.call-start
  51.5 0.9 copy-done.5
  52.4 1.5 collective-permute-start
  53.9 20.4 %collective-permute-done = bf16[1,128,1536]{2,1,0:T(8,128)(2,1)S(1)} collective-permute-done((bf16[1,128,1536]{2,1,0:T(8,128)(2,1)S(1)}, bf16[1,128,1536]{2,1,0:T(8,128)(2,1)S(1)}, u32[]{:S(2)}, u32[]{:S(2)}) %collective-permute-start) | collective-permute-done | bytes 393248 | tf_op jit(solution)/shard_map/ppermute | solution.py:20
  74.3 1.6 collective-permute-start.1
  76.0 21.4 %collective-permute-done.1 = bf16[1,128,1536]{2,1,0:T(8,128)(2,1)S(1)} collective-permute-done((bf16[1,128,1536]{2,1,0:T(8,128)(2,1)S(1)}, bf16[1,128,1536]{2,1,0:T(8,128)(2,1)S(1)}, u32[]{:S(2)}, u32[]{:S(2)}) %collective-permute-start.1) | collective-permute-done | bytes 393248 | tf_op jit(solution)/shard_map/ppermute | solution.py:20
  97.4 0.0 collective-permute-start.2
  97.4 0.0 copy-done.6
  97.4 0.2 copy.22
  97.6 0.0 copy-start.2
  97.6 14.9 %collective-permute-done.2 = bf16[1,128,1536]{2,1,0:T(8,128)(2,1)S(1)} collective-permute-done((bf16[1,128,1536]{2,1,0:T(8,128)(2,1)S(1)}, bf16[1,128,1536]{2,1,0:T(8,128)(2,1)S(1)}, u32[]{:S(2)}, u32[]{:S(2)}) %collective-permute-start.2) | collective-permute-done | bytes 393248 | tf_op jit(solution)/shard_map/ppermute | solution.py:20
  112.6 0.2 maximum_bitcast_fusion
  112.8 1.8 gather_fusion
  114.6 2.7 copy.27
  117.3 0.6 reshape_squeeze_reshape_transpose.3
  118.0 0.0 copy-start
  118.0 0.0 all-gather.4.cloned.1.call-done
  118.0 0.0 copy-done.2
  118.0 2.7 multiply_reduce_fusion
  120.7 1.0 exponential_reduce_fusion
  121.7 0.5 exponential_convert_fusion
  122.2 39.5 %reduce-scatter.4.cloned.1.call-done = f32[128,1536]{1,0:T(8,128)} async-done(((f32[512,1536]{1,0:T(8,128)}), f32[128,1536]{1,0:T(8,128)}) %reduce-scatter.4.cloned.1.call-update) | async-done | bytes 786448 | tf_op jit(solution)/shard_map/reduce_scatter | solution.py:57
  161.7 1.9 convert_element_type.58
  163.7 1.2 copy.26
  164.9 0.0 copy-done
  164.9 1.3 multiply_reduce_fusion.1
  166.2 0.0 all-gather.8.cloned.1.call-update
  166.2 0.0 reduce-scatter.6.cloned.1.call-start
  166.3 0.0 copy-start.3
  166.3 2.1 multiply_convert_fusion.1
  168.4 0.0 copy-done.3
  168.4 1.7 multiply_convert_fusion
  170.1 2.6 copy.30
  172.8 0.0 reduce-scatter.6.cloned.1.call-update
  172.8 0.0 reduce-scatter.8.cloned.1.call-start
  172.8 1.7 convolution_convert_fusion.2
  174.5 2.6 copy.31
  177.1 0.0 reduce-scatter.8.cloned.1.call-update
  177.2 0.0 all-reduce.3.cloned.1.call-start
  177.2 0.8 copy-done.7
  178.0 20.2 %all_gather.15 = bf16[1,512,364]{1,2,0:T(8,128)(2,1)S(1)} all-gather(bf16[1,128,364]{1,2,0:T(8,128)(2,1)S(1)} %copy-done.7), channel_id=1, replica_groups=mesh['dp'=2,'row'=4,'col'=4] {'col'}, dimensions={1}, use_global_device_ids=true | all-gather | bytes 465920 | tf_op jit(solution)/shard_map/all_gather | solution.py:40
  198.3 4.6 convolution_convert_fusion.1
  202.9 4.5 all-gather.8.cloned.1.call-done
  207.3 9.3 %convolution_convert_fusion = bf16[1536,3072]{1,0:T(8,128)(2,1)} fusion(bf16[1,512,3072]{2,1,0:T(8,128)(2,1)} %all-gather.6.cloned.1.call-done, bf16[1,512,1536]{1,2,0:T(8,128)(2,1)} %all-gather.8.cloned.1.call-done), kind=kOutput, calls=%fused_computation.1 | convolution fusion | flops 4836556800 | bytes 14155776 | tf_op jit(solution)/shard_map/dot_general | solution.py:27
  216.7 0.0 all-reduce.3.cloned.1.call-update
  216.7 1.4 copy-done.1
  218.1 1.5 convolution_multiply_fusion
  219.5 2.3 copy.32
  221.8 21.2 %reduce-scatter.6.cloned.1.call-done = bf16[128,1536]{1,0:T(8,128)(2,1)} async-done(((bf16[512,1536]{1,0:T(8,128)(2,1)}), bf16[128,1536]{1,0:T(8,128)(2,1)}) %reduce-scatter.6.cloned.1.call-update) | async-done | bytes 393232 | tf_op jit(solution)/shard_map/reduce_scatter | solution.py:86
  243.0 2.0 bitcast_convert_fusion.1
  245.0 34.5 %reduce-scatter.8.cloned.1.call-done = bf16[128,1536]{1,0:T(8,128)(2,1)} async-done(((bf16[512,1536]{1,0:T(8,128)(2,1)}), bf16[128,1536]{1,0:T(8,128)(2,1)}) %reduce-scatter.8.cloned.1.call-update) | async-done | bytes 393232 | tf_op jit(solution)/shard_map/reduce_scatter | solution.py:92
  279.5 2.0 bitcast_convert_fusion
  281.4 270.0 %all-reduce.3.cloned.1.call-done = (bf16[1536,3072]{1,0:T(8,128)(2,1)}, bf16[364,3072]{1,0:T(8,128)(2,1)}) async-done(((bf16[1536,3072]{1,0:T(8,128)(2,1)}, bf16[364,3072]{1,0:T(8,128)(2,1)}), (bf16[1536,3072]{1,0:T(8,128)(2,1)}, bf16[364,3072]{1,0:T(8,128)(2,1)})) %all-reduce.3.cloned.1.call-update) | async-done | bytes 11673616 | tf_op jit(solution)/shard_map/psum | solution.py:102
  551.4 12.9 %convert_element_type.71 = f32[1536,3072]{1,0:T(8,128)} convert(bf16[1536,3072]{1,0:T(8,128)(2,1)} %get-tuple-element.15) | non-fusion elementwise | flops 4718592 | bytes 28311552 | tf_op jit(solution)/shard_map/convert_element_type | solution.py:102
  564.3 2.7 convert_element_type.73
  (9 shorter events, 0.0 us)
Async XLA Ops:
  7.2 33.7 %all-gather.6.cloned.1.call-start = ((), (), s32[]{:S(2)}) async-start(), calls=%async_computation.4 | async-start | bytes 3932160 | tf_op jit(solution)/shard_map/all_gather | solution.py:56
  7.9 110.1 %all-gather.4.cloned.1.call-start = ((), (), s32[]{:S(2)}) async-start(), calls=%async_computation.3 | async-start | bytes 1966080 | tf_op jit(solution)/shard_map/all_gather | solution.py:38
  9.9 151.9 %reduce-scatter.4.cloned.1.call-start = ((), (), s32[]{:S(2)}) async-start(), calls=%async_computation.5 | async-start | bytes 3932160 | tf_op jit(solution)/shard_map/reduce_scatter | solution.py:57
  51.4 1.0 copy-start.5
  51.4 46.0 %copy-start.6 = (bf16[1,128,1536]{2,1,0:T(8,128)(2,1)S(1)}, bf16[1,128,1536]{2,1,0:T(8,128)(2,1)}, u32[]{:S(2)}) copy-start(bf16[1,128,1536]{2,1,0:T(8,128)(2,1)} %param.7) | copy-start | bytes 1179652
  51.4 155.9 %all-gather.8.cloned.1.call-start = ((), (), s32[]{:S(2)}) async-start(), calls=%async_computation.8 | async-start | bytes 1966080 | tf_op jit(solution)/shard_map/all_gather | solution.py:77
  52.4 21.9 %collective-permute-start = (bf16[1,128,1536]{2,1,0:T(8,128)(2,1)S(1)}, bf16[1,128,1536]{2,1,0:T(8,128)(2,1)S(1)}, u32[]{:S(2)}, u32[]{:S(2)}) collective-permute-start(bf16[1,128,1536]{2,1,0:T(8,128)(2,1)S(1)} %copy-done.5), channel_id=1, source_target_pairs={{0,1},{1,2},{2,3},{3,0},{4,5},{5,6},{6,7},{7,4},{8,9},{9,10},{10,1... | collective-permute-start | bytes 1179656 | tf_op jit(solution)/shard_map/ppermute | solution.py:20
  74.3 23.0 %collective-permute-start.1 = (bf16[1,128,1536]{2,1,0:T(8,128)(2,1)S(1)}, bf16[1,128,1536]{2,1,0:T(8,128)(2,1)S(1)}, u32[]{:S(2)}, u32[]{:S(2)}) collective-permute-start(bf16[1,128,1536]{2,1,0:T(8,128)(2,1)S(1)} %collective-permute-done), channel_id=1, source_target_pairs={{0,1},{1,2},{2,3},{3,0},{4,5},{5,6},{6,7},{7,4},{8,9},{9,10},{10,1... | collective-permute-start | bytes 1179656 | tf_op jit(solution)/shard_map/ppermute | solution.py:20
  97.4 15.2 %collective-permute-start.2 = (bf16[1,128,1536]{2,1,0:T(8,128)(2,1)S(1)}, bf16[1,128,1536]{2,1,0:T(8,128)(2,1)S(1)}, u32[]{:S(2)}, u32[]{:S(2)}) collective-permute-start(bf16[1,128,1536]{2,1,0:T(8,128)(2,1)S(1)} %collective-permute-done.1), channel_id=1, source_target_pairs={{0,1},{1,2},{2,3},{3,0},{4,5},{5,6},{6,7},{7,4},{8,9},{9,10},{10,1... | collective-permute-start | bytes 1179656 | tf_op jit(solution)/shard_map/ppermute | solution.py:20
  97.6 20.4 %copy-start.2 = (bf16[1,128,1536]{1,2,0:T(8,128)(2,1)}, bf16[1,128,1536]{1,2,0:T(8,128)(2,1)S(1)}, u32[]{:S(2)}) copy-start(bf16[1,128,1536]{1,2,0:T(8,128)(2,1)S(1)} %copy.22) | copy-start | bytes 1179652
  118.0 46.9 %copy-start = (bf16[512,12,128]{0,2,1:T(8,128)(2,1)}, bf16[512,12,128]{0,2,1:T(8,128)(2,1)S(1)}, u32[]{:S(2)}) copy-start(bf16[512,12,128]{0,2,1:T(8,128)(2,1)S(1)} %reshape_squeeze_reshape_transpose.3) | copy-start | bytes 4718596
  166.2 76.8 %reduce-scatter.6.cloned.1.call-start = ((), (), s32[]{:S(2)}) async-start(), calls=%async_computation.6 | async-start | bytes 1966080 | tf_op jit(solution)/shard_map/reduce_scatter | solution.py:86
  166.3 2.1 copy-start.3
  172.8 106.7 %reduce-scatter.8.cloned.1.call-start = ((), (), s32[]{:S(2)}) async-start(), calls=%async_computation.7 | async-start | bytes 1966080 | tf_op jit(solution)/shard_map/reduce_scatter | solution.py:92
  177.1 0.9 copy-start.7
  177.2 374.3 %all-reduce.3.cloned.1.call-start = ((), (), s32[]{:S(2)}) async-start(), calls=%async_computation.9 | async-start | bytes 23396352 | tf_op jit(solution)/shard_map/psum | solution.py:102
  216.7 1.4 copy-start.1
  551.4 12.9 %copy-start.4 = (bf16[364,3072]{1,0:T(8,128)(2,1)S(1)}, bf16[364,3072]{1,0:T(8,128)(2,1)}, u32[]{:S(2)}) copy-start(bf16[364,3072]{1,0:T(8,128)(2,1)} %get-tuple-element.16) | copy-start | bytes 6709252
Sparse Core Ops, SparseCore 0:
  9.6 31.2 all-gather.5
  43.0 52.9 all-gather.3
  98.8 62.8 reduce-scatter.3
  166.4 40.9 all-gather.7
  209.5 33.4 reduce-scatter.5
  245.2 34.2 reduce-scatter.7
  282.6 268.8 all-reduce.2
